TPU v7x, 32 devices: a whole 2x2x4 slice. The times are simulated.
32 devices in a mesh: uv: 8 (over z, y), tm: 4 (over x, core).
Axes of the slice: x: 2, y: 2, z: 4, core: 2. Of those that a mesh axis runs over, the one named last changes fastest.
Arguments:
- visibility: bfloat16 [4, 1024, 2048], P('tm', 'uv'), may hold values from -1536 to 1536
- anchor: int32 [4, 1024], P('tm', 'uv'), may hold values from 0 to 80
- offset: int32 [4, 1024], P('tm', 'uv'), may hold values from 0 to 63
- slot_rows: int32 [4, 8, 8, 32], P('tm', 'uv'), may hold values from 0 to 127, as said below
- counts: int32 [4, 8, 8], P('tm', 'uv'), may hold values from 0 to 32, as said below
Outputs:
- delay: float32 [2048, 2048], P(('uv', 'tm'))
Inputs may be any that keep to these rules, and one draw needn't show every extreme that they name: For every g and s the first counts[g, s, d] entries of slot_rows[g, s, d] over all d name each of the 128 rows of device s exactly once; entries at slots k >= counts[g, s, d] are arbitrary rows and are not used. counts[g, s, :] sums to 128; in each time group one tile receives 32 rows from every device and another tile none; the other tiles come in pairs whose counts from one device sum to 32.
All inputs are finite; a program needn't handle non-finite values.
Results may differ from a plain program's by a relative error of at most 0.0047.
Values may be sent and summed in bfloat16 or wider, within the bound.
No kernel may reach another device: no remote copies, remote signals or barrier semaphores. Data moves between devices by JAX's collectives and lax.ppermute only.
A program may use at most 64 MiB of HBM per device.

v0:
```python
import math
import jax
import jax.numpy as jnp
from jax import lax
from jax.sharding import PartitionSpec as P

NCH = 1024
ROWS_DEV = 128
TS = 16
KTAPS = 8
OSAMP = 8


def kernel_taps(offsets):
    tap_index = jnp.arange(KTAPS, dtype=jnp.float32)
    sub_shift = (offsets.astype(jnp.float32) + 0.5) / OSAMP
    distance = tap_index[None, :] - (KTAPS / 2 - 1.0) - sub_shift[:, None]
    return jnp.exp(-distance * distance / (2.0 * 1.2 * 1.2))


def tap_matrix(cell_ids, anchors, offsets):
    span = TS - KTAPS + 1
    anchor_y = anchors // span
    anchor_x = anchors % span
    taps_y = kernel_taps(offsets // OSAMP)
    taps_x = kernel_taps(offsets % OSAMP)
    cell_y = cell_ids // TS
    cell_x = cell_ids % TS
    along_y = jnp.zeros((cell_ids.shape[0], anchors.shape[0]), jnp.float32)
    along_x = jnp.zeros((cell_ids.shape[0], anchors.shape[0]), jnp.float32)
    for step in range(KTAPS):
        along_y = along_y + jnp.where(
            cell_y[:, None] == anchor_y[None, :] + step, taps_y[None, :, step], 0.0
        )
        along_x = along_x + jnp.where(
            cell_x[:, None] == anchor_x[None, :] + step, taps_x[None, :, step], 0.0
        )
    return (along_y * along_x).astype(jnp.bfloat16)


def delay_table():
    freq = jnp.arange(NCH, dtype=jnp.int32)
    phase = freq[:, None] * freq[None, :] % NCH
    angle = 2.0 * math.pi / NCH * phase.astype(jnp.float32)
    cosine = jnp.cos(angle)
    sine = jnp.sin(angle)
    window_arg = 2.0 * math.pi * freq.astype(jnp.float32) / (NCH - 1)
    taper = (
        0.35875
        - 0.48829 * jnp.cos(window_arg)
        + 0.14128 * jnp.cos(2.0 * window_arg)
        - 0.01168 * jnp.cos(3.0 * window_arg)
    )
    tap_cos = taper[:, None] * cosine
    tap_sin = taper[:, None] * sine
    upper = jnp.concatenate([tap_cos, -tap_sin], axis=1)
    lower = jnp.concatenate([tap_sin, tap_cos], axis=1)
    return jnp.concatenate([upper, lower], axis=0).astype(jnp.bfloat16)


def per_device(visibility, anchor, offset, slot_rows, counts):
    time_groups = lax.axis_size("tm")
    cell_share = TS * TS // time_groups
    vis_rows = visibility[0]
    row_width = vis_rows.shape[1]
    slot_table = slot_rows[0, 0]
    tile_count, slot_depth = slot_table.shape
    is_live = (jnp.arange(slot_depth, dtype=jnp.int32)[None, :] < counts[0, 0][:, None]).reshape(-1)
    flat_index = slot_table.reshape(-1)
    outgoing = jnp.where(
        is_live[:, None], jnp.take(vis_rows, flat_index, axis=0), jnp.zeros((), vis_rows.dtype)
    )
    outgoing = outgoing.reshape(tile_count, slot_depth, row_width)
    out_anchor = jnp.take(anchor[0], flat_index).reshape(tile_count, slot_depth)
    out_offset = jnp.take(offset[0], flat_index).reshape(tile_count, slot_depth)
    arrived, arr_anchor, arr_offset = (
        lax.all_to_all(outgoing, "uv", split_axis=0, concat_axis=0, tiled=True),
        lax.all_to_all(out_anchor, "uv", split_axis=0, concat_axis=0, tiled=True),
        lax.all_to_all(out_offset, "uv", split_axis=0, concat_axis=0, tiled=True),
    )
    my_start = lax.axis_index("tm") * cell_share
    all_cells = jnp.arange(TS * TS, dtype=jnp.int32)
    weights = tap_matrix(all_cells, arr_anchor.reshape(-1), arr_offset.reshape(-1))
    flat_vis = arrived.reshape(-1, row_width)
    full_sum = lax.psum(jnp.dot(weights, flat_vis, preferred_element_type=jnp.float32), "tm")
    summed = lax.dynamic_slice_in_dim(full_sum, my_start, cell_share, 0)
    grid = summed.astype(jnp.bfloat16)
    transform = delay_table()
    out_scale = 4.0 / math.sqrt(NCH * time_groups * ROWS_DEV)
    return jnp.dot(grid, transform, preferred_element_type=jnp.float32) * out_scale


def solution(mesh):
    in_specs = (
        P("tm", "uv", None),
        P("tm", "uv"),
        P("tm", "uv"),
        P("tm", "uv", None, None),
        P("tm", "uv", None),
    )
    out_specs = P(("uv", "tm"), None)
    return jax.shard_map(
        per_device, mesh=mesh, in_specs=in_specs, out_specs=out_specs, check_vma=False
    )
```

profile of v0, /device:TPU:0, one launch (start us, length us, event | category | flops | bytes accessed | tf_op | source)
XLA Modules:
  0.0 105.8 jit_solution(13739666395043265725)
XLA Ops:
  0.0 0.0 copy-start
  0.0 0.8 reshape_squeeze.7
  0.9 1.9 %gather_fusion.2 = s32[256]{0:T(256)S(1)} fusion(s32[128]{0:T(128)} %bitcast.33, s32[1024]{0:T(1024)S(1)} %pad_clamp_fusion.1), kind=kCustom, calls=%fused_computation.1.clone | custom fusion | bytes 3072 | tf_op jit(solution)/shard_map/jit(_take)/gather | solution.py:75
  2.7 1.9 %gather_fusion.1 = s32[256]{0:T(256)S(1)} fusion(s32[128]{0:T(128)} %bitcast.34, s32[1024]{0:T(1024)S(1)} %pad_clamp_fusion.1), kind=kCustom, calls=%fused_computation.clone | custom fusion | bytes 3072 | tf_op jit(solution)/shard_map/jit(_take)/gather | solution.py:74
  4.7 0.7 all_to_all.17
  5.3 7.3 %all-to-all-start.1 = ((s32[8,1,32]{2,1,0:T(1,128)}), s32[8,1,32]{2,1,0:T(1,128)S(1)}, u32[]{:S(2)}, u32[]{:S(2)}) async-start(s32[8,1,32]{2,1,0:T(1,128)} %all_to_all.17), calls=%async_computation.1 | async-start | bytes 8192 | tf_op jit(solution)/shard_map/all_to_all | solution.py:79
  12.6 0.0 copy-done.2
  12.6 0.1 reshape_squeeze.9
  12.7 0.1 multiply_subtract_fusion
  12.8 0.0 copy-done.3
  12.8 0.1 iota_compare_fusion
  12.9 0.0 copy-done
  12.9 1.4 %gather_fusion = bf16[256,2048]{1,0:T(8,128)(2,1)S(1)} fusion(bf16[128,2048]{1,0:T(8,128)(2,1)S(1)} %bitcast.32, s32[1024]{0:T(1024)S(1)} %pad_clamp_fusion), kind=kCustom, calls=%fused_computation.2 | custom fusion | bytes 2098176 | tf_op jit(solution)/shard_map/jit(_take)/gather | solution.py:71
  14.2 1.2 %select_select_fusion = bf16[8,32,2048]{2,1,0:T(8,128)(2,1)} fusion(bf16[8,32,2048]{2,1,0:T(8,128)(2,1)S(1)} %bitcast.35, pred[8,32]{1,0:T(8,128)(4,1)S(1)} %get-tuple-element.60, pred[8,32]{1,0:T(8,128)(4,1)S(1)} %get-tuple-element.59), kind=kLoop, calls=%fused_computation.25 | loop fusion | flops 1048576 | bytes 2097664 | tf_op jit(solution)/shard_map/jit(_where)/select_n | solution.py:70
  15.4 0.7 all_to_all.15
  16.1 2.9 %all-to-all-done.1 = s32[8,1,32]{2,1,0:T(1,128)S(1)} async-done(((s32[8,1,32]{2,1,0:T(1,128)}), s32[8,1,32]{2,1,0:T(1,128)S(1)}, u32[]{:S(2)}, u32[]{:S(2)}) %all-to-all-start.1) | async-done | bytes 1056 | tf_op jit(solution)/shard_map/all_to_all | solution.py:79
  19.0 3.2 %all-to-all-start = ((s32[8,1,32]{2,1,0:T(1,128)}), s32[8,1,32]{2,1,0:T(1,128)S(1)}, u32[]{:S(2)}, u32[]{:S(2)}) async-start(s32[8,1,32]{2,1,0:T(1,128)} %all_to_all.15), calls=%async_computation | async-start | bytes 8192 | tf_op jit(solution)/shard_map/all_to_all | solution.py:78
  22.3 6.4 %all-to-all-done = s32[8,1,32]{2,1,0:T(1,128)S(1)} async-done(((s32[8,1,32]{2,1,0:T(1,128)}), s32[8,1,32]{2,1,0:T(1,128)S(1)}, u32[]{:S(2)}, u32[]{:S(2)}) %all-to-all-start) | async-done | bytes 1056 | tf_op jit(solution)/shard_map/all_to_all | solution.py:78
  28.7 3.6 %all-to-all-start.2 = ((bf16[8,32,2048]{2,1,0:T(8,128)(2,1)}), bf16[8,32,2048]{2,1,0:T(8,128)(2,1)S(1)}, u32[]{:S(2)}, u32[]{:S(2)}) async-start(bf16[8,32,2048]{2,1,0:T(8,128)(2,1)} %select_select_fusion), calls=%async_computation.2 | async-start | bytes 2097152 | tf_op jit(solution)/shard_map/all_to_all | solution.py:77
  32.2 19.1 %negate_convert_fusion = (bf16[1024,1024]{1,0:T(8,128)(2,1)}, bf16[1024,1024]{1,0:T(8,128)(2,1)}, bf16[1024,1024]{1,0:T(8,128)(2,1)}) fusion(f32[1024]{0:T(1024)S(1)} %multiply_subtract_fusion), kind=kLoop, calls=%fused_computation.17 | loop fusion | flops 20971520 | bytes 6295552 | tf_op jit(solution)/shard_map/convert.5
  51.3 0.5 broadcast.585
  51.8 0.7 reduce.13
  52.5 0.1 reshape.340
  52.6 0.1 ne.248
  52.7 0.1 div.91
  52.8 0.1 rem.188
  52.9 0.1 fusion.55
  53.0 3.3 %all-to-all-done.2 = bf16[8,32,2048]{2,1,0:T(8,128)(2,1)S(1)} async-done(((bf16[8,32,2048]{2,1,0:T(8,128)(2,1)}), bf16[8,32,2048]{2,1,0:T(8,128)(2,1)S(1)}, u32[]{:S(2)}, u32[]{:S(2)}) %all-to-all-start.2) | async-done | bytes 1048608 | tf_op jit(solution)/shard_map/all_to_all | solution.py:77
  56.3 1.0 copy-done.1
  57.3 2.1 %fusion.18 = f32[256,2048]{1,0:T(8,128)S(1)} fusion(bf16[256,2048]{1,0:T(8,128)(2,1)} %bitcast.36, f32[256]{0:T(256)S(1)} %bitcast.52, s32[256]{0:T(256)S(1)} %get-tuple-element.46, f32[256]{0:T(256)S(1)} %bitcast.51, s32[256]{0:T(256)S(1)} %get-tuple-element.42, f32[256]{0:T(256)S(1)} %bitcast.50, s32[256]{0:T(256)S(1)} %get-tuple-element.43, ...), kind=kOutput, calls=%fused_computation.28 | convolution fusion | flops 271581184 | bytes 3180544 | tf_op jit(solution)/shard_map/dot_general | solution.py:85
  59.4 40.5 %all-reduce.1 = bf16[256,2048]{1,0:T(8,128)(2,1)} all-reduce(f32[256,2048]{1,0:T(8,128)S(1)} %fusion.18), channel_id=1, replica_groups=mesh['uv'=8,'tm'=4] {'tm'}, use_global_device_ids=true, to_apply=%region_0.0 | all-reduce | flops 524288 | bytes 3145728 | tf_op jit(solution)/shard_map/psum | solution.py:85
  99.9 5.9 %fusion.15 = f32[64,2048]{1,0:T(8,128)} fusion(bf16[1024,1024]{1,0:T(8,128)(2,1)} %get-tuple-element.30, bf16[1024,1024]{1,0:T(8,128)(2,1)} %get-tuple-element.29, bf16[1024,1024]{1,0:T(8,128)(2,1)} %get-tuple-element.28, bf16[256,2048]{1,0:T(8,128)(2,1)} %all-reduce.1, s32[]{:T(128)S(6)} %select_n.242), kind=kOutput, calls=%fused_computation.24 | convolution fusion | flops 570556416 | bytes 7077892 | tf_op jit(solution)/shard_map/dot_general | solution.py:90
  (16 shorter events, 0.2 us)
Async XLA Ops:
  0.0 12.9 %copy-start = (bf16[1,128,2048]{2,1,0:T(8,128)(2,1)S(1)}, bf16[1,128,2048]{2,1,0:T(8,128)(2,1)}, u32[]{:S(2)}) copy-start(bf16[1,128,2048]{2,1,0:T(8,128)(2,1)} %param.7) | copy-start | bytes 1572868
  0.0 12.6 %copy-start.2 = (s32[1,1,8,32]{3,2,1,0:T(8,128)S(1)}, s32[1,1,8,32]{3,2,1,0:T(8,128)}, u32[]{:S(2)}) copy-start(s32[1,1,8,32]{3,2,1,0:T(8,128)} %param.10) | copy-start | bytes 3076
  0.0 12.8 %copy-start.3 = (s32[1,1,8]{2,1,0:T(1,128)S(1)}, s32[1,1,8]{2,1,0:T(1,128)}, u32[]{:S(2)}) copy-start(s32[1,1,8]{2,1,0:T(1,128)} %param.11) | copy-start | bytes 100
  5.3 13.7 %all-to-all-start.1 = ((s32[8,1,32]{2,1,0:T(1,128)}), s32[8,1,32]{2,1,0:T(1,128)S(1)}, u32[]{:S(2)}, u32[]{:S(2)}) async-start(s32[8,1,32]{2,1,0:T(1,128)} %all_to_all.17), calls=%async_computation.1 | async-start | bytes 8192 | tf_op jit(solution)/shard_map/all_to_all | solution.py:79
  19.0 9.7 %all-to-all-start = ((s32[8,1,32]{2,1,0:T(1,128)}), s32[8,1,32]{2,1,0:T(1,128)S(1)}, u32[]{:S(2)}, u32[]{:S(2)}) async-start(s32[8,1,32]{2,1,0:T(1,128)} %all_to_all.15), calls=%async_computation | async-start | bytes 8192 | tf_op jit(solution)/shard_map/all_to_all | solution.py:78
  28.7 27.6 %all-to-all-start.2 = ((bf16[8,32,2048]{2,1,0:T(8,128)(2,1)}), bf16[8,32,2048]{2,1,0:T(8,128)(2,1)S(1)}, u32[]{:S(2)}, u32[]{:S(2)}) async-start(bf16[8,32,2048]{2,1,0:T(8,128)(2,1)} %select_select_fusion), calls=%async_computation.2 | async-start | bytes 2097152 | tf_op jit(solution)/shard_map/all_to_all | solution.py:77
  56.3 1.0 copy-start.1
where the time goes:
time: 106 us
  blocking collectives  40.5 us (38%)
  other arithmetic  21.3 us (20%)
  starting transfers between devices  14.1 us (13%)
  waiting for transfers between devices  12.6 us (12%)
  local copies, waits for them, and re-layouts  9.27 us (9%)
  matrix products  7.99 us (8%)
    psum x1, blocking collectives, per_device(): lax.psum(jnp.dot(weights, flat_vis, preferred_element_type=jnp.float32),...  40.5 us
    another operation x1, other arithmetic  19.1 us
    all_to_all x1, starting transfers between devices, per_device(): lax.all_to_all(out_offset, 'uv', split_axis=0, concat_axis=0, tiled=True)  7.28 us
    all_to_all x1, waiting for transfers between devices, per_device(): lax.all_to_all(out_anchor, 'uv', split_axis=0, concat_axis=0, tiled=True)  6.38 us
    dot_general x1, matrix products, per_device(): jnp.dot(grid, transform, preferred_element_type=jnp.float32) * out_scale  5.92 us
    all_to_all x1, starting transfers between devices, per_device(): lax.all_to_all(outgoing, 'uv', split_axis=0, concat_axis=0, tiled=True)  3.56 us
    all_to_all x1, waiting for transfers between devices, per_device(): lax.all_to_all(outgoing, 'uv', split_axis=0, concat_axis=0, tiled=True)  3.3 us
    all_to_all x1, starting transfers between devices, per_device(): lax.all_to_all(out_anchor, 'uv', split_axis=0, concat_axis=0, tiled=True)  3.25 us
  transfers between devices with their start and end apart: 3, of which 3 were waited for; matrix products, arithmetic and copies ran while one was open for 22% of the time, Pallas kernels for 0%

commit v1 on v0

--- a/solution.py
+++ b/solution.py
@@ -82,7 +82,9 @@
     all_cells = jnp.arange(TS * TS, dtype=jnp.int32)
     weights = tap_matrix(all_cells, arr_anchor.reshape(-1), arr_offset.reshape(-1))
     flat_vis = arrived.reshape(-1, row_width)
-    full_sum = lax.psum(jnp.dot(weights, flat_vis, preferred_element_type=jnp.float32), "tm")
+    x = jnp.dot(weights, flat_vis, preferred_element_type=jnp.float32)
+    blocks = lax.all_gather(x, "tm")
+    full_sum = jnp.sum(blocks, axis=0)
     summed = lax.dynamic_slice_in_dim(full_sum, my_start, cell_share, 0)
     grid = summed.astype(jnp.bfloat16)
     transform = delay_table()

time: 106 us -> 149 us (1.41)
  waiting for transfers between devices: 12.6 us -> 69 us
  blocking collectives: 40.5 us -> 0 us
  between operations: 0.12 us -> 13.5 us
  matrix products: 7.99 us -> 15.8 us
  other arithmetic: 21.3 us -> 26.8 us
    psum x1 -> x0, blocking collectives: 40.5 us -> none  [per_device(): lax.psum(jnp.dot(weights, flat_vis, preferred_element_type=jnp.float32),...]
    all_gather x0 -> x1, waiting for transfers between devices: none -> 38.9 us  [per_device(): blocks = lax.all_gather(x, 'tm')]
    all_to_all x1, waiting for transfers between devices: 3.3 us -> 22.1 us  [per_device(): lax.all_to_all(outgoing, 'uv', split_axis=0, concat_axis=0, tiled=True)]
    dot_general x1, matrix products: 5.92 us -> 13.6 us  [per_device(): jnp.dot(grid, transform, preferred_element_type=jnp.float32) * out_scale]
    reduce_sum x0 -> x1, other arithmetic: none -> 5.53 us  [per_device(): full_sum = jnp.sum(blocks, axis=0)]
    all_to_all x1, starting transfers between devices: 3.25 us -> 7.28 us  [per_device(): lax.all_to_all(out_anchor, 'uv', split_axis=0, concat_axis=0, tiled=True)]
    all_to_all x1, starting transfers between devices: 7.28 us -> 3.31 us  [per_device(): lax.all_to_all(out_offset, 'uv', split_axis=0, concat_axis=0, tiled=True)]
    all_to_all x1, waiting for transfers between devices: 6.38 us -> 2.86 us  [per_device(): lax.all_to_all(out_anchor, 'uv', split_axis=0, concat_axis=0, tiled=True)]
  transfers between devices with their start and end apart: 3 -> 4, of which waited for: 3 -> 4; matrix products, arithmetic and copies ran while one was open for 22% -> 16% of each run, Pallas kernels for 0% -> 0%
where the time goes in v1:
time: 149 us; the launch traced here: 148 us
  waiting for transfers between devices  69 us (46%)
  other arithmetic  26.8 us (18%)
  matrix products  15.8 us (11%)
  starting transfers between devices  14.4 us (10%)
  between operations  13.5 us (9%)
  local copies, waits for them, and re-layouts  8.95 us (6%)
    all_gather x1, waiting for transfers between devices, per_device(): blocks = lax.all_gather(x, 'tm')  38.9 us
    all_to_all x1, waiting for transfers between devices, per_device(): lax.all_to_all(outgoing, 'uv', split_axis=0, concat_axis=0, tiled=True)  22.1 us
    another operation x1, other arithmetic  18.4 us
    dot_general x1, matrix products, per_device(): jnp.dot(grid, transform, preferred_element_type=jnp.float32) * out_scale  13.6 us
    all_to_all x1, starting transfers between devices, per_device(): lax.all_to_all(out_anchor, 'uv', split_axis=0, concat_axis=0, tiled=True)  7.28 us
    reduce_sum x1, other arithmetic, per_device(): full_sum = jnp.sum(blocks, axis=0)  5.53 us
    all_to_all x1, waiting for transfers between devices, per_device(): lax.all_to_all(out_offset, 'uv', split_axis=0, concat_axis=0, tiled=True)  5.15 us
    all_to_all x1, starting transfers between devices, per_device(): lax.all_to_all(outgoing, 'uv', split_axis=0, concat_axis=0, tiled=True)  3.56 us
  transfers between devices with their start and end apart: 4, of which 4 were waited for; matrix products, arithmetic and copies ran while one was open for 16% of the time, Pallas kernels for 0%

profile of v1, /device:TPU:0, one launch (start us, length us, event | category | flops | bytes accessed | tf_op | source)
XLA Modules:
  0.0 148.4 jit_solution(8674068299946302563)
XLA Ops:
  6.5 0.0 copy-start
  6.5 0.8 reshape_squeeze.7
  7.4 1.9 %gather_fusion.1 = s32[256]{0:T(256)S(1)} fusion(s32[128]{0:T(128)} %bitcast.34, s32[1024]{0:T(1024)S(1)} %pad_clamp_fusion.1), kind=kCustom, calls=%fused_computation.clone | custom fusion | bytes 3072 | tf_op jit(solution)/shard_map/jit(_take)/gather | solution.py:74
  9.3 1.9 %gather_fusion.2 = s32[256]{0:T(256)S(1)} fusion(s32[128]{0:T(128)} %bitcast.35, s32[1024]{0:T(1024)S(1)} %pad_clamp_fusion.1), kind=kCustom, calls=%fused_computation.1.clone | custom fusion | bytes 3072 | tf_op jit(solution)/shard_map/jit(_take)/gather | solution.py:75
  11.2 0.7 all_to_all.15
  11.9 7.3 %all-to-all-start = ((s32[8,1,32]{2,1,0:T(1,128)}), s32[8,1,32]{2,1,0:T(1,128)S(1)}, u32[]{:S(2)}, u32[]{:S(2)}) async-start(s32[8,1,32]{2,1,0:T(1,128)} %all_to_all.15), calls=%async_computation | async-start | bytes 8192 | tf_op jit(solution)/shard_map/all_to_all | solution.py:78
  19.1 0.8 reshape_squeeze.9
  19.9 0.8 iota_compare_fusion
  20.7 0.7 all_to_all.17
  21.4 0.0 copy-done
  21.4 1.4 gather_fusion
  22.7 2.9 %all-to-all-done = s32[8,1,32]{2,1,0:T(1,128)S(1)} async-done(((s32[8,1,32]{2,1,0:T(1,128)}), s32[8,1,32]{2,1,0:T(1,128)S(1)}, u32[]{:S(2)}, u32[]{:S(2)}) %all-to-all-start) | async-done | bytes 1056 | tf_op jit(solution)/shard_map/all_to_all | solution.py:78
  25.6 3.3 %all-to-all-start.1 = ((s32[8,1,32]{2,1,0:T(1,128)}), s32[8,1,32]{2,1,0:T(1,128)S(1)}, u32[]{:S(2)}, u32[]{:S(2)}) async-start(s32[8,1,32]{2,1,0:T(1,128)} %all_to_all.17), calls=%async_computation.1 | async-start | bytes 8192 | tf_op jit(solution)/shard_map/all_to_all | solution.py:79
  28.9 1.2 select_select_fusion
  30.1 5.1 %all-to-all-done.1 = s32[8,1,32]{2,1,0:T(1,128)S(1)} async-done(((s32[8,1,32]{2,1,0:T(1,128)}), s32[8,1,32]{2,1,0:T(1,128)S(1)}, u32[]{:S(2)}, u32[]{:S(2)}) %all-to-all-start.1) | async-done | bytes 1056 | tf_op jit(solution)/shard_map/all_to_all | solution.py:79
  35.3 3.6 %all-to-all-start.2 = ((bf16[8,32,2048]{2,1,0:T(8,128)(2,1)}), bf16[8,32,2048]{2,1,0:T(8,128)(2,1)S(1)}, u32[]{:S(2)}, u32[]{:S(2)}) async-start(bf16[8,32,2048]{2,1,0:T(8,128)(2,1)} %select_select_fusion), calls=%async_computation.2 | async-start | bytes 2097152 | tf_op jit(solution)/shard_map/all_to_all | solution.py:77
  38.8 0.2 all-gather.3.cloned.1.call-start
  39.1 0.1 div.91
  39.2 0.1 rem.188
  39.3 0.1 ne.248
  39.4 0.5 broadcast.585
  39.9 0.7 reduce.13
  40.6 0.1 reshape.340
  40.7 0.1 fusion.55
  40.8 22.1 %all-to-all-done.2 = bf16[8,32,2048]{2,1,0:T(8,128)(2,1)S(1)} async-done(((bf16[8,32,2048]{2,1,0:T(8,128)(2,1)}), bf16[8,32,2048]{2,1,0:T(8,128)(2,1)S(1)}, u32[]{:S(2)}, u32[]{:S(2)}) %all-to-all-start.2) | async-done | bytes 1048608 | tf_op jit(solution)/shard_map/all_to_all | solution.py:77
  62.9 2.2 %fusion.18 = f32[256,2048]{1,0:T(8,128)} fusion(bf16[256,2048]{1,0:T(8,128)(2,1)S(1)} %bitcast.38, f32[256]{0:T(256)S(1)} %bitcast.54, s32[256]{0:T(256)S(1)} %get-tuple-element.46, f32[256]{0:T(256)S(1)} %bitcast.53, s32[256]{0:T(256)S(1)} %get-tuple-element.42, f32[256]{0:T(256)S(1)} %bitcast.52, s32[256]{0:T(256)S(1)} %get-tuple-element.43, ...), kind=kOutput, calls=%fused_computation.28 | convolution fusion | flops 271581184 | bytes 3180544 | tf_op jit(solution)/shard_map/dot_general | solution.py:85
  65.1 0.0 all-gather.3.cloned.1.call-update
  65.1 0.1 multiply_subtract_fusion
  65.2 18.4 %negate_convert_fusion = (bf16[1024,1024]{1,0:T(8,128)(2,1)S(1)}, bf16[1024,1024]{1,0:T(8,128)(2,1)}, bf16[1024,1024]{1,0:T(8,128)(2,1)}) fusion(f32[1024]{0:T(1024)S(1)} %multiply_subtract_fusion), kind=kLoop, calls=%fused_computation.17 | loop fusion | flops 20971520 | bytes 6295552 | tf_op jit(solution)/shard_map/convert.5
  83.6 38.9 %all-gather.3.cloned.1.call-done = f32[1024,2048]{1,0:T(8,128)} async-done(((f32[256,2048]{1,0:T(8,128)}), f32[1024,2048]{1,0:T(8,128)}) %all-gather.3.cloned.1.call-update) | async-done | bytes 8388624 | tf_op jit(solution)/shard_map/all_gather | solution.py:86
  122.4 5.5 %reduce_sum.9 = bf16[256,2048]{1,0:T(8,128)(2,1)} reduce(f32[4,256,2048]{2,1,0:T(8,128)} %bitcast.36, f32[]{:T(128)} %constant.137.clone.1), dimensions={0}, to_apply=%region_0.0 | reduce | flops 1572864 | bytes 9437188 | tf_op jit(solution)/shard_map/reduce_sum | solution.py:87
  128.0 13.6 %fusion.15 = f32[64,2048]{1,0:T(8,128)} fusion(bf16[1024,1024]{1,0:T(8,128)(2,1)} %get-tuple-element.30, bf16[1024,1024]{1,0:T(8,128)(2,1)} %get-tuple-element.29, bf16[1024,1024]{1,0:T(8,128)(2,1)S(1)} %get-tuple-element.28, bf16[256,2048]{1,0:T(8,128)(2,1)} %reduce_sum.9, s32[]{:T(128)S(6)} %select_n.242), kind=kOutput, calls=%fused_computation.24 | convolution fusion | flops 570556416 | bytes 7077892 | tf_op jit(solution)/shard_map/dot_general | solution.py:92
  (13 shorter events, 0.2 us)
Async XLA Ops:
  6.5 14.8 %copy-start = (bf16[1,128,2048]{2,1,0:T(8,128)(2,1)S(1)}, bf16[1,128,2048]{2,1,0:T(8,128)(2,1)}, u32[]{:S(2)}) copy-start(bf16[1,128,2048]{2,1,0:T(8,128)(2,1)} %param.7) | copy-start | bytes 1572868
  11.9 13.7 %all-to-all-start = ((s32[8,1,32]{2,1,0:T(1,128)}), s32[8,1,32]{2,1,0:T(1,128)S(1)}, u32[]{:S(2)}, u32[]{:S(2)}) async-start(s32[8,1,32]{2,1,0:T(1,128)} %all_to_all.15), calls=%async_computation | async-start | bytes 8192 | tf_op jit(solution)/shard_map/all_to_all | solution.py:78
  25.6 9.6 %all-to-all-start.1 = ((s32[8,1,32]{2,1,0:T(1,128)}), s32[8,1,32]{2,1,0:T(1,128)S(1)}, u32[]{:S(2)}, u32[]{:S(2)}) async-start(s32[8,1,32]{2,1,0:T(1,128)} %all_to_all.17), calls=%async_computation.1 | async-start | bytes 8192 | tf_op jit(solution)/shard_map/all_to_all | solution.py:79
  35.3 27.6 %all-to-all-start.2 = ((bf16[8,32,2048]{2,1,0:T(8,128)(2,1)}), bf16[8,32,2048]{2,1,0:T(8,128)(2,1)S(1)}, u32[]{:S(2)}, u32[]{:S(2)}) async-start(bf16[8,32,2048]{2,1,0:T(8,128)(2,1)} %select_select_fusion), calls=%async_computation.2 | async-start | bytes 2097152 | tf_op jit(solution)/shard_map/all_to_all | solution.py:77
  38.8 83.6 %all-gather.3.cloned.1.call-start = ((), (), s32[]{:S(2)}) async-start(), calls=%async_computation.3 | async-start | bytes 10485760 | tf_op jit(solution)/shard_map/all_gather | solution.py:86
Sparse Core Ops, SparseCore 0:
  65.2 57.1 all-gather.2
